TPU v7x, 512 devices: a whole 4x8x8 slice. The times are simulated.
512 devices in a mesh: dp: 8 (over z), cent: 64 (over x, y, core).
Axes of the slice: x: 4, y: 8, z: 8, core: 2. Of those that a mesh axis runs over, the one named last changes fastest.
Arguments:
- points: bfloat16 [24576, 1024], P(('dp', 'cent')), may hold values from -6 to 6
- assign: int32 [24576], P(('dp', 'cent')), may hold values from 0 to 32767, as said below
- centroids: float32 [32768, 1024], P('cent'), may hold values from -6 to 6
- counts: int32 [32768], P('cent'), may hold values from 1 to 4
Outputs:
- new_centroids: float32 [32768, 1024], P('cent')
- best: float32 [24576], P(('dp', 'cent'))
Inputs may be any that keep to these rules, and one draw needn't show every extreme that they name: `assign`: split the points into aligned blocks of 3072 points in order (the points of one dp index). In every block, the clusters k * 512 to (k + 1) * 512 - 1 receive exactly 48 points together, for every k.
All inputs are finite; a program needn't handle non-finite values.
Results may differ from a plain program's by a relative error of at most 0.0003.
Values may be sent and summed in bfloat16 or wider, within the bound.
No kernel may reach another device: no remote copies, remote signals or barrier semaphores. Data moves between devices by JAX's collectives and lax.ppermute only.
A program may use at most 128 MiB of HBM per device.

v0:
```python
import jax
import jax.numpy as jnp
from jax import lax
from jax.sharding import PartitionSpec as P


def renorm(merged):
    return merged * lax.rsqrt(jnp.mean(merged * merged, axis=1, keepdims=True) + 1e-05)


def cluster_terms(rows, labels, kdev):
    first = lax.axis_index("cent") * kdev
    local = labels - first
    onehot = (local[None, :] == jnp.arange(kdev, dtype=jnp.int32)[:, None]).astype(jnp.bfloat16)
    return jnp.dot(onehot, rows, preferred_element_type=jnp.float32)


def per_device(points, assign, centroids, counts):
    kdev = centroids.shape[0]
    pdev = points.shape[0]
    weighted = centroids * counts.astype(jnp.float32)[:, None]
    rows, labels = (
        lax.all_gather(points, "cent", axis=0, tiled=True),
        lax.all_gather(assign, "cent", axis=0, tiled=True),
    )
    sums = cluster_terms(rows, labels, kdev)
    total = lax.psum(sums, "dp")
    fresh = renorm(weighted + total)
    rounded = fresh.astype(jnp.bfloat16)
    scores = jnp.dot(rows, rounded.T, preferred_element_type=jnp.float32)
    local_best = jnp.max(scores, axis=1)
    merged_best = lax.pmax(local_best, "cent")
    top = lax.dynamic_slice_in_dim(merged_best, lax.axis_index("cent") * pdev, pdev, 0)
    values = points.astype(jnp.float32)
    width = points.shape[1]
    scale = width * jnp.sqrt(jnp.mean(values * values, axis=1) + 1e-06)
    return (fresh, top / scale)


def solution(mesh):
    placed = (P(("dp", "cent"), None), P(("dp", "cent")), P("cent", None), P("cent"))
    return jax.shard_map(
        per_device,
        mesh=mesh,
        in_specs=placed,
        out_specs=(P("cent", None), P(("dp", "cent"))),
        check_vma=False,
    )
```

profile of v0, /device:TPU:64, one launch (start us, length us, event | category | flops | bytes accessed | tf_op | source)
XLA Modules:
  0.0 617.8 jit_solution(2940238520247544569)
XLA Ops:
  7.2 0.0 all-gather.2.cloned.1.call-start
  7.2 0.7 all-gather.2.cloned.1.call-update
  7.9 0.0 all-reduce.3.cloned.1.call-start
  7.9 1.3 dynamic-slice
  9.9 0.9 dynamic-update-slice
  10.8 251.6 %all-reduce = s32[3072]{0:T(1024)S(1)} all-reduce(s32[3072]{0:T(1024)S(1)} %dynamic-update-slice), channel_id=1, replica_groups=mesh['dp'=8,'cent'=64] {'cent'}, use_global_device_ids=true, to_apply=%add | all-reduce | flops 3072 | bytes 24576
  262.4 0.0 all-gather.2.cloned.1.call-done
  262.4 0.0 copy-start.3
  262.4 7.5 %fusion = f32[512,1024]{1,0:T(8,128)} fusion(bf16[3072,1024]{1,0:T(8,128)(2,1)} %all-gather.2.cloned.1.call-done, s32[3072]{0:T(1024)S(1)} %broadcast_subtract_fusion), kind=kOutput, calls=%fused_computation.1 | convolution fusion | flops 3222798336 | bytes 8400896 | tf_op jit(solution)/shard_map/dot_general | solution.py:15
  269.9 0.0 all-reduce.3.cloned.1.call-update
  269.9 0.7 copy-done.4
  270.6 0.0 copy-done.3
  270.6 0.1 multiply_reduce_fusion.1
  270.7 83.2 %all-reduce.3.cloned.1.call-done = f32[512,1024]{1,0:T(8,128)} async-done(((f32[512,1024]{1,0:T(8,128)}), f32[512,1024]{1,0:T(8,128)}) %all-reduce.3.cloned.1.call-update) | async-done | bytes 2097168 | tf_op jit(solution)/shard_map/psum | solution.py:27
  353.9 0.0 copy-done
  353.9 2.2 multiply_reduce_fusion
  356.1 0.1 copy-done.1
  356.1 0.4 broadcast_multiply_fusion
  356.5 0.0 copy-start.2
  356.5 1.3 copy-done.2
  357.8 1.8 copy-done.5
  359.7 3.7 convolution_reduce_fusion
  363.4 247.0 %pmax.7 = f32[3072]{0:T(1024)S(1)} all-reduce(f32[3072]{0:T(1024)S(1)} %convolution_reduce_fusion), channel_id=1, replica_groups=mesh['dp'=8,'cent'=64] {'cent'}, use_global_device_ids=true, to_apply=%region_3.0 | all-reduce | flops 3072 | bytes 24576 | tf_op jit(solution)/shard_map/pmax | solution.py:32
  610.4 0.6 multiply_divide_fusion
  (8 shorter events, 0.0 us)
Async XLA Ops:
  7.2 255.2 %all-gather.2.cloned.1.call-start = ((), (), s32[]{:S(2)}) async-start(), calls=%async_computation | async-start | bytes 6389760 | tf_op jit(solution)/shard_map/all_gather | solution.py:23
  7.9 346.0 %all-reduce.3.cloned.1.call-start = ((), (), s32[]{:S(2)}) async-start(), calls=%async_computation.1 | async-start | bytes 4194304 | tf_op jit(solution)/shard_map/psum | solution.py:27
  262.4 8.2 %copy-start.3 = (bf16[48,1024]{1,0:T(8,128)(2,1)S(1)}, bf16[48,1024]{1,0:T(8,128)(2,1)}, u32[]{:S(2)}) copy-start(bf16[48,1024]{1,0:T(8,128)(2,1)} %param.4) | copy-start | bytes 294916
  269.9 0.7 copy-start.4
  269.9 84.0 %copy-start = (f32[512,1024]{1,0:T(8,128)S(1)}, f32[512,1024]{1,0:T(8,128)}, u32[]{:S(2)}) copy-start(f32[512,1024]{1,0:T(8,128)} %param.6) | copy-start | bytes 6291460
  353.9 2.2 copy-start.1
  356.1 3.5 copy-start.5
  356.5 1.3 copy-start.2
Sparse Core Ops, SparseCore 0:
  11.3 89.7 all-gather.1
  270.1 83.7 all-reduce.2
where the time goes:
time: 618 us
  blocking collectives  499 us (81%)
  waiting for transfers between devices  83.9 us (14%)
  between operations  14.7 us (2%)
  matrix products  11.3 us (2%)
    unnamed x1, blocking collectives  252 us
    pmax x1, blocking collectives, per_device(): merged_best = lax.pmax(local_best, 'cent')  247 us
    psum x1, waiting for transfers between devices, per_device(): total = lax.psum(sums, 'dp')  83.2 us
  transfers between devices with their start and end apart: 2, of which 1 were waited for; matrix products, arithmetic and copies ran while one was open for 0% of the time, Pallas kernels for 0%

commit v1 on v0

--- a/solution.py
+++ b/solution.py
@@ -1,7 +1,15 @@
+import functools
 import jax
 import jax.numpy as jnp
 from jax import lax
 from jax.sharding import PartitionSpec as P
+
+
+def enter_frame(inner_x, group_axis):
+    return lax.all_gather(inner_x, group_axis).sum(axis=0)
+
+
+recover_domain = functools.partial(enter_frame, group_axis="dp")
 
 
 def renorm(merged):
@@ -24,7 +32,7 @@
         lax.all_gather(assign, "cent", axis=0, tiled=True),
     )
     sums = cluster_terms(rows, labels, kdev)
-    total = lax.psum(sums, "dp")
+    total = recover_domain(sums)
     fresh = renorm(weighted + total)
     rounded = fresh.astype(jnp.bfloat16)
     scores = jnp.dot(rows, rounded.T, preferred_element_type=jnp.float32)

time: 618 us -> 717 us (1.16)
  waiting for transfers between devices: 83.9 us -> 170 us
  other arithmetic: 3.25 us -> 11.4 us
    all_gather x0 -> x1, waiting for transfers between devices: none -> 169 us  [enter_frame(): return lax.all_gather(inner_x, group_axis).sum(axis=0)]
    psum x1 -> x0, waiting for transfers between devices: 83.2 us -> none  [per_device(): total = lax.psum(sums, 'dp')]
    reduce_sum x0 -> x1, other arithmetic: none -> 8.06 us  [enter_frame(): return lax.all_gather(inner_x, group_axis).sum(axis=0)]
where the time goes in v1:
time: 717 us
  blocking collectives  502 us (70%)
  waiting for transfers between devices  170 us (24%)
  between operations  14.8 us (2%)
  matrix products  14 us (2%)
  other arithmetic  11.4 us (2%)
    unnamed x1, blocking collectives  252 us
    pmax x1, blocking collectives, per_device(): merged_best = lax.pmax(local_best, 'cent')  250 us
    all_gather x1, waiting for transfers between devices, enter_frame(): return lax.all_gather(inner_x, group_axis).sum(axis=0)  169 us
  transfers between devices with their start and end apart: 2, of which 1 were waited for; matrix products, arithmetic and copies ran while one was open for 0% of the time, Pallas kernels for 0%

profile of v1, /device:TPU:64, one launch (start us, length us, event | category | flops | bytes accessed | tf_op | source)
XLA Modules:
  0.0 716.5 jit_solution(1433299862973145970)
XLA Ops:
  7.2 0.0 all-gather.4.cloned.1.call-start
  7.2 0.7 all-gather.4.cloned.1.call-update
  7.9 0.0 all-gather.6.cloned.1.call-start
  7.9 1.3 dynamic-slice
  9.9 0.9 dynamic-update-slice
  10.8 251.7 %all-reduce = s32[3072]{0:T(1024)S(1)} all-reduce(s32[3072]{0:T(1024)S(1)} %dynamic-update-slice), channel_id=1, replica_groups=mesh['dp'=8,'cent'=64] {'cent'}, use_global_device_ids=true, to_apply=%add | all-reduce | flops 3072 | bytes 24576
  262.4 0.0 all-gather.4.cloned.1.call-done
  262.4 7.5 %fusion = f32[512,1024]{1,0:T(8,128)} fusion(bf16[3072,1024]{1,0:T(8,128)(2,1)} %all-gather.4.cloned.1.call-done, s32[3072]{0:T(1024)S(1)} %broadcast_subtract_fusion), kind=kOutput, calls=%fused_computation.1 | convolution fusion | flops 3222798336 | bytes 8400896 | tf_op jit(solution)/shard_map/dot_general | solution.py:23
  269.9 0.0 copy-start.3
  269.9 0.0 all-gather.6.cloned.1.call-update
  270.0 0.7 copy-done.3
  270.6 0.2 copy-done.2
  270.8 0.1 multiply_reduce_fusion.1
  271.0 169.3 %all-gather.6.cloned.1.call-done = f32[4096,1024]{1,0:T(8,128)} async-done(((f32[512,1024]{1,0:T(8,128)}), f32[4096,1024]{1,0:T(8,128)}) %all-gather.6.cloned.1.call-update) | async-done | bytes 16777232 | tf_op jit(solution)/shard_map/all_gather | solution.py:9
  440.2 8.1 %reduce_sum.27 = f32[512,1024]{1,0:T(8,128)S(1)} reduce(f32[8,512,1024]{2,1,0:T(8,128)} %bitcast.4, f32[]{:T(128)} %constant.4.clone.1), dimensions={0}, to_apply=%region_0.0 | reduce | flops 3670016 | bytes 18874372 | tf_op jit(solution)/shard_map/reduce_sum | solution.py:9
  448.3 0.0 copy-start
  448.3 2.2 multiply_reduce_fusion
  450.5 0.0 copy-done
  450.5 0.4 broadcast_multiply_fusion
  450.9 0.0 copy-start.1
  450.9 1.3 copy-done.1
  452.3 6.5 convolution_reduce_fusion
  458.8 250.3 %pmax.7 = f32[3072]{0:T(1024)S(1)} all-reduce(f32[3072]{0:T(1024)S(1)} %convolution_reduce_fusion), channel_id=1, replica_groups=mesh['dp'=8,'cent'=64] {'cent'}, use_global_device_ids=true, to_apply=%region_3.0 | all-reduce | flops 3072 | bytes 24576 | tf_op jit(solution)/shard_map/pmax | solution.py:40
  709.1 0.6 multiply_divide_fusion
  (5 shorter events, 0.0 us)
Async XLA Ops:
  7.2 255.2 %all-gather.4.cloned.1.call-start = ((), (), s32[]{:S(2)}) async-start(), calls=%async_computation | async-start | bytes 6389760 | tf_op jit(solution)/shard_map/all_gather | solution.py:31
  7.9 432.3 %all-gather.6.cloned.1.call-start = ((), (), s32[]{:S(2)}) async-start(), calls=%async_computation.1 | async-start | bytes 18874368 | tf_op jit(solution)/shard_map/all_gather | solution.py:9
  269.9 0.7 copy-start.3
  269.9 0.9 copy-start.2
  448.3 2.2 copy-start
  450.9 1.3 copy-start.1
Sparse Core Ops, SparseCore 0:
  11.3 89.7 all-gather.3
  270.1 170.1 all-gather.5
